TPU v7x, 256 devices: a whole 4x4x8 slice. The times are simulated.
256 devices in a mesh: req: 32 (over z, x_lo, core), tp: 8 (over x_hi, y).
Axes of the slice: x: 4 (x_hi: 2, x_lo: 2; x = x_hi * 2 + x_lo), y: 4, z: 8, core: 2. Of those that a mesh axis runs over, the one named last changes fastest.
Arguments:
- queries: bfloat16 [12288, 8192], P('req', 'tp'), may hold values from -40 to 40
- suffix_kv: bfloat16 [2, 12288, 1024], P(None, 'req', 'tp'), may hold values from -4 to 4
- prefix_kv: bfloat16 [2, 32, 256, 1024], P(None, 'req', 'tp'), may hold values from -4 to 4
- suffix_length: int32 [31], replicated, may hold values from 16 to 384, as said below
- request_group: int32 [31], replicated, may hold values from 0 to 3
- request_order: int32 [31], replicated, may hold values from 0 to 30, each once
- owner_map: int32 [32], replicated, may hold values from 0 to 31, each once
Outputs:
- attention: bfloat16 [12288, 8192], P('req', 'tp')
Inputs may be any that keep to these rules, and one draw needn't show every extreme that they name: `suffix_length`: every suffix has 16 to 384 tokens; in every draw one suffix has exactly 384 tokens and one exactly 16.
All inputs are finite; a program needn't handle non-finite values.
Results may differ from a plain program's by a relative error of at most 0.007.
Values may be sent and summed in bfloat16 or wider, within the bound.
No kernel may reach another device: no remote copies, remote signals or barrier semaphores. Data moves between devices by JAX's collectives and lax.ppermute only.
A program may use at most 128 MiB of HBM per device.

v0:
```python
import math

import jax
import jax.numpy as jnp
from jax import lax
from jax.sharding import PartitionSpec as P

QH = 64
KVH = 8
HD = 128
GROUPS = 4


masked_score = -1e30


def from_behind(block, axis, distance):
    devices = range(lax.axis_size(axis))
    route = [(i - distance, i) for i in devices if i - distance in devices]
    return lax.ppermute(block, axis, route)


def pack_index(slot_ids, starts, stops):
    inside = (starts[None, :] <= slot_ids[:, None]) & (slot_ids[:, None] < stops[None, :])
    request_ids = jnp.arange(starts.shape[0], dtype=jnp.int32)
    found = jnp.sum(jnp.where(inside, request_ids[None, :], 0), axis=1)
    missing = jnp.where(jnp.any(inside, axis=1), 0, starts.shape[0]).astype(jnp.int32)
    return found + missing


def pick_rows(lookup, selector, extent):
    matches = selector[:, None] == jnp.arange(extent, dtype=jnp.int32)[None, :]
    return jnp.sum(jnp.where(matches, lookup[None, :], 0), axis=1)


def per_device(
    queries, suffix_kv, prefix_kv, suffix_length, request_group, request_order, owner_map
):
    tok_rows = queries.shape[0]
    head_cols = suffix_kv.shape[2]
    kv_heads = head_cols // HD
    per_kv = QH // KVH
    stored_count = owner_map.shape[0]
    per_group = stored_count // GROUPS
    requests = suffix_length.shape[0]
    score_scale = 1.0 / math.sqrt(HD)
    packed_length = pick_rows(suffix_length, request_order, requests)
    packed_group = pick_rows(request_group, request_order, requests)
    starts = (jnp.arange(requests, dtype=jnp.int32) + 1) * tok_rows - packed_length // 2
    stops = starts + packed_length
    device = lax.axis_index("req")
    slot_ids = device * tok_rows + jnp.arange(tok_rows, dtype=jnp.int32)
    own_pack = pack_index(slot_ids, starts, stops)
    is_live = own_pack < requests
    slot_group = pick_rows(packed_group, own_pack, requests)
    block_ids = jnp.arange(stored_count, dtype=jnp.int32)
    stored_group = jnp.sum(
        jnp.where(owner_map[None, :] == block_ids[:, None], (block_ids // per_group)[None, :], 0),
        axis=1,
    )
    query_heads = queries.reshape(tok_rows, kv_heads, per_kv, HD)

    def absorb(carried, key_rows, value_rows, allowed):
        running_max, running_sum, running_acc = carried
        scores = (
            jnp.einsum("tjqd,kjd->jtqk", query_heads, key_rows, preferred_element_type=jnp.float32)
            * score_scale
        )
        visible = allowed[None, :, None, :]
        scores = jnp.where(visible, scores, masked_score)
        new_max = jnp.maximum(running_max, jnp.max(scores, axis=-1))
        weights = jnp.where(visible, jnp.exp(scores - new_max[..., None]), 0.0)
        shrink = jnp.exp(running_max - new_max)
        new_sum = running_sum * shrink + jnp.sum(weights, axis=-1)
        product = jnp.einsum(
            "jtqk,kjd->jtqd",
            weights.astype(jnp.bfloat16),
            value_rows,
            preferred_element_type=jnp.float32,
        )
        return (new_max, new_sum, running_acc * shrink[..., None] + product)

    earlier = from_behind(suffix_kv, "req", 1)
    nearby = jnp.concatenate([earlier, suffix_kv], axis=1)
    near_slots = device * tok_rows - tok_rows + jnp.arange(2 * tok_rows, dtype=jnp.int32)
    near_pack = pack_index(near_slots, starts, stops)
    near_allowed = (
        (near_pack[None, :] == own_pack[:, None])
        & (near_slots[None, :] <= slot_ids[:, None])
        & (near_slots[None, :] >= 0)
        & is_live[:, None]
    )
    initial = (
        jnp.full((kv_heads, tok_rows, per_kv), masked_score, jnp.float32),
        jnp.zeros((kv_heads, tok_rows, per_kv), jnp.float32),
        jnp.zeros((kv_heads, tok_rows, per_kv, HD), jnp.float32),
    )
    carried = absorb(
        initial,
        nearby[0].reshape(2 * tok_rows, kv_heads, HD),
        nearby[1].reshape(2 * tok_rows, kv_heads, HD),
        near_allowed,
    )
    stored = lax.all_gather(prefix_kv, "req", axis=1, tiled=True)
    relaid = lax.all_to_all(stored, "tp", split_axis=3, concat_axis=2, tiled=True)
    status = carried
    extent = relaid.shape[1]
    block_rows = relaid.shape[2]
    stride = math.gcd(extent, max(1, 512 // block_rows))
    passes = extent // stride
    key_rows = relaid[0].reshape(passes, stride * block_rows, kv_heads, HD)
    value_rows = relaid[1].reshape(passes, stride * block_rows, kv_heads, HD)
    key_groups = jnp.repeat(stored_group, block_rows).reshape(passes, stride * block_rows)

    def visit_block(inner, inputs):
        keys_here, values_here, groups_here = inputs
        allowed = (groups_here[None, :] == slot_group[:, None]) & is_live[:, None]
        inner = absorb(inner, keys_here, values_here, allowed)
        return (inner, None)

    status, unused = lax.scan(visit_block, status, (key_rows, value_rows, key_groups))
    carried = status
    running_max, running_sum, running_acc = carried
    divisor = jnp.where(is_live[None, :, None], running_sum, 1.0)
    result = jnp.where(is_live[None, :, None, None], running_acc / divisor[..., None], 0.0)
    return (
        jnp.transpose(result, (1, 0, 2, 3))
        .reshape(tok_rows, kv_heads * per_kv * HD)
        .astype(jnp.bfloat16)
    )


def solution(mesh):
    in_specs = (
        P("req", "tp"),
        P(None, "req", "tp"),
        P(None, "req", "tp", None),
        P(),
        P(),
        P(),
        P(),
    )
    out_specs = P("req", "tp")
    return jax.shard_map(
        per_device, mesh=mesh, in_specs=in_specs, out_specs=out_specs, check_vma=False
    )
```

profile of v0, /device:TPU:1, one launch (start us, length us, event | category | flops | bytes accessed | tf_op | source)
XLA Modules:
  0.0 346.6 jit_solution(16441505130025673132)
XLA Ops:
  7.3 4.5 %collective-permute-start = (bf16[2,384,128]{2,1,0:T(8,128)(2,1)}, bf16[2,384,128]{2,1,0:T(8,128)(2,1)S(1)}, u32[]{:S(2)}, u32[]{:S(2)}) collective-permute-start(bf16[2,384,128]{2,1,0:T(8,128)(2,1)} %param.10), channel_id=1, source_target_pairs={{0,8},{8,16},{16,24},{24,32},{32,40},{40,48},{48,56},{56,64},{64,7... | collective-permute-start | bytes 589832 | tf_op jit(solution)/shard_map/ppermute | solution.py:20
  15.8 64.1 %all-gather.2.cloned.1.call-done = bf16[2,32,32,1024]{3,2,0,1:T(8,128)(2,1)} async-done(((bf16[2,1,32,1024]{3,2,0,1:T(8,128)(2,1)}), bf16[2,32,32,1024]{3,2,0,1:T(8,128)(2,1)}) %all-gather.2.cloned.1.call-update) | async-done | bytes 4194320 | tf_op jit(solution)/shard_map/all_gather | solution.py:104
  79.9 23.2 %copy.43 = bf16[2,32,32,1024]{2,1,0,3:T(8,128)(2,1)} copy(bf16[2,32,32,1024]{3,2,0,1:T(8,128)(2,1)} %all-gather.2.cloned.1.call-done) | data formatting | bytes 8388608 | tf_op jit(solution)/shard_map/all_gather | solution.py:104
  103.1 18.7 %reshape.344 = bf16[8,2,131072]{2,1,0:T(2,128)(2,1)} reshape(bf16[1024,2,32,32]{3,2,1,0:T(8,128)(2,1)} %bitcast.120) | data formatting | bytes 8388608
  121.8 6.3 %all-to-all-start = ((bf16[8,2,131072]{2,1,0:T(2,128)(2,1)}), bf16[8,2,131072]{2,1,0:T(2,128)(2,1)}, u32[]{:S(2)}, u32[]{:S(2)}) async-start(bf16[8,2,131072]{2,1,0:T(2,128)(2,1)} %reshape.344), calls=%async_computation | async-start | bytes 8388608 | tf_op jit(solution)/shard_map/all_to_all | solution.py:105
  137.1 39.8 %all-to-all-done = bf16[8,2,131072]{2,1,0:T(2,128)(2,1)} async-done(((bf16[8,2,131072]{2,1,0:T(2,128)(2,1)}), bf16[8,2,131072]{2,1,0:T(2,128)(2,1)}, u32[]{:S(2)}, u32[]{:S(2)}) %all-to-all-start) | async-done | bytes 4194336 | tf_op jit(solution)/shard_map/all_to_all | solution.py:105
  176.8 12.4 %reshape.345 = bf16[1024,2,32,32]{3,2,1,0:T(8,128)(2,1)} reshape(bf16[8,2,131072]{2,1,0:T(2,128)(2,1)} %all-to-all-done) | data formatting | bytes 8388608
  189.3 12.6 %fusion.40 = (bf16[1,32,8,32,128]{3,1,0,4,2:T(8,128)(2,1)}, bf16[1,32,8,32,128]{3,1,0,4,2:T(8,128)(2,1)}) fusion(bf16[2,32,8,32,128]{3,1,0,4,2:T(8,128)(2,1)} %bitcast.121), kind=kLoop, calls=%fused_computation.80 | loop fusion | bytes 8388608 | tf_op jit(solution)/shard_map/slice | solution.py:112
  201.8 8.5 %copy.44 = bf16[1,32,8,32,128]{4,3,2,1,0:T(8,128)(2,1)S(1)} copy(bf16[1,32,8,32,128]{3,1,0,4,2:T(8,128)(2,1)} %get-tuple-element.131) | data formatting | bytes 4194304 | tf_op jit(solution)/shard_map/slice | solution.py:111
  210.3 9.3 %copy.46 = bf16[1,32,8,32,128]{4,3,2,1,0:T(8,128)(2,1)} copy(bf16[1,32,8,32,128]{3,1,0,4,2:T(8,128)(2,1)} %get-tuple-element.130) | data formatting | bytes 4194304 | tf_op jit(solution)/shard_map/slice | solution.py:112
  219.7 116.5 %while.14 = (s32[]{:T(128)}, f32[1,384,8]{1,2,0:T(8,128)S(1)}, f32[1,384,8]{1,2,0:T(8,128)S(1)}, f32[1,384,8,128]{3,1,2,0:T(8,128)}, s32[16,512]{1,0:T(8,128)S(1...) while((s32[]{:T(128)}, f32[1,384,8]{1,2,0:T(8,128)S(1)}, ...), condition=%wide.region_13.14_spmd, body=%wide.region_10.13_spmd.sunk | while | flops 826942464 | bytes 24060404 | solution.py:121
  221.0 4.4 %bitcast_add_fusion.6 = f32[1,384,8,128]{3,1,2,0:T(8,128)} fusion(f32[1,384,8,128]{3,1,2,0:T(8,128)} %get-tuple-element.220, f32[512,384,8]{1,0,2:T(8,128)S(1)} %get-tuple-element.204, f32[384,8]{0,1:T(8,128)S(1)} %bitcast.122, pred[384,512]{0,1:T(8,128)(4,1)S(1)} %compare_and_fusion.4, f32[384,8]{0,1:T(8,128)S(1)} %get-tuple-element.205, ...), kind=kOutput, calls=%fused_computation.7.clone.1 | convolution fusion | flops 411303936 | bytes 9789952 | tf_op jit(solution)/shard_map/while/body/eval_jaxpr/jtqk,kjd->jtqd/dot_general | solution.py:75
  228.3 4.4 %bitcast_add_fusion.6 = f32[1,384,8,128]{3,1,2,0:T(8,128)} fusion(f32[1,384,8,128]{3,1,2,0:T(8,128)} %get-tuple-element.220, f32[512,384,8]{1,0,2:T(8,128)S(1)} %get-tuple-element.204, f32[384,8]{0,1:T(8,128)S(1)} %bitcast.122, pred[384,512]{0,1:T(8,128)(4,1)S(1)} %compare_and_fusion.4, f32[384,8]{0,1:T(8,128)S(1)} %get-tuple-element.205, ...), kind=kOutput, calls=%fused_computation.7.clone.1 | convolution fusion | flops 411303936 | bytes 9789952 | tf_op jit(solution)/shard_map/while/body/eval_jaxpr/jtqk,kjd->jtqd/dot_general | solution.py:75
  235.6 4.4 %bitcast_add_fusion.6 = f32[1,384,8,128]{3,1,2,0:T(8,128)} fusion(f32[1,384,8,128]{3,1,2,0:T(8,128)} %get-tuple-element.220, f32[512,384,8]{1,0,2:T(8,128)S(1)} %get-tuple-element.204, f32[384,8]{0,1:T(8,128)S(1)} %bitcast.122, pred[384,512]{0,1:T(8,128)(4,1)S(1)} %compare_and_fusion.4, f32[384,8]{0,1:T(8,128)S(1)} %get-tuple-element.205, ...), kind=kOutput, calls=%fused_computation.7.clone.1 | convolution fusion | flops 411303936 | bytes 9789952 | tf_op jit(solution)/shard_map/while/body/eval_jaxpr/jtqk,kjd->jtqd/dot_general | solution.py:75
  242.9 4.4 %bitcast_add_fusion.6 = f32[1,384,8,128]{3,1,2,0:T(8,128)} fusion(f32[1,384,8,128]{3,1,2,0:T(8,128)} %get-tuple-element.220, f32[512,384,8]{1,0,2:T(8,128)S(1)} %get-tuple-element.204, f32[384,8]{0,1:T(8,128)S(1)} %bitcast.122, pred[384,512]{0,1:T(8,128)(4,1)S(1)} %compare_and_fusion.4, f32[384,8]{0,1:T(8,128)S(1)} %get-tuple-element.205, ...), kind=kOutput, calls=%fused_computation.7.clone.1 | convolution fusion | flops 411303936 | bytes 9789952 | tf_op jit(solution)/shard_map/while/body/eval_jaxpr/jtqk,kjd->jtqd/dot_general | solution.py:75
  250.2 4.4 %bitcast_add_fusion.6 = f32[1,384,8,128]{3,1,2,0:T(8,128)} fusion(f32[1,384,8,128]{3,1,2,0:T(8,128)} %get-tuple-element.220, f32[512,384,8]{1,0,2:T(8,128)S(1)} %get-tuple-element.204, f32[384,8]{0,1:T(8,128)S(1)} %bitcast.122, pred[384,512]{0,1:T(8,128)(4,1)S(1)} %compare_and_fusion.4, f32[384,8]{0,1:T(8,128)S(1)} %get-tuple-element.205, ...), kind=kOutput, calls=%fused_computation.7.clone.1 | convolution fusion | flops 411303936 | bytes 9789952 | tf_op jit(solution)/shard_map/while/body/eval_jaxpr/jtqk,kjd->jtqd/dot_general | solution.py:75
  257.4 4.4 %bitcast_add_fusion.6 = f32[1,384,8,128]{3,1,2,0:T(8,128)} fusion(f32[1,384,8,128]{3,1,2,0:T(8,128)} %get-tuple-element.220, f32[512,384,8]{1,0,2:T(8,128)S(1)} %get-tuple-element.204, f32[384,8]{0,1:T(8,128)S(1)} %bitcast.122, pred[384,512]{0,1:T(8,128)(4,1)S(1)} %compare_and_fusion.4, f32[384,8]{0,1:T(8,128)S(1)} %get-tuple-element.205, ...), kind=kOutput, calls=%fused_computation.7.clone.1 | convolution fusion | flops 411303936 | bytes 9789952 | tf_op jit(solution)/shard_map/while/body/eval_jaxpr/jtqk,kjd->jtqd/dot_general | solution.py:75
  264.7 4.4 %bitcast_add_fusion.6 = f32[1,384,8,128]{3,1,2,0:T(8,128)} fusion(f32[1,384,8,128]{3,1,2,0:T(8,128)} %get-tuple-element.220, f32[512,384,8]{1,0,2:T(8,128)S(1)} %get-tuple-element.204, f32[384,8]{0,1:T(8,128)S(1)} %bitcast.122, pred[384,512]{0,1:T(8,128)(4,1)S(1)} %compare_and_fusion.4, f32[384,8]{0,1:T(8,128)S(1)} %get-tuple-element.205, ...), kind=kOutput, calls=%fused_computation.7.clone.1 | convolution fusion | flops 411303936 | bytes 9789952 | tf_op jit(solution)/shard_map/while/body/eval_jaxpr/jtqk,kjd->jtqd/dot_general | solution.py:75
  272.0 4.4 %bitcast_add_fusion.6 = f32[1,384,8,128]{3,1,2,0:T(8,128)} fusion(f32[1,384,8,128]{3,1,2,0:T(8,128)} %get-tuple-element.220, f32[512,384,8]{1,0,2:T(8,128)S(1)} %get-tuple-element.204, f32[384,8]{0,1:T(8,128)S(1)} %bitcast.122, pred[384,512]{0,1:T(8,128)(4,1)S(1)} %compare_and_fusion.4, f32[384,8]{0,1:T(8,128)S(1)} %get-tuple-element.205, ...), kind=kOutput, calls=%fused_computation.7.clone.1 | convolution fusion | flops 411303936 | bytes 9789952 | tf_op jit(solution)/shard_map/while/body/eval_jaxpr/jtqk,kjd->jtqd/dot_general | solution.py:75
  279.3 4.4 %bitcast_add_fusion.6 = f32[1,384,8,128]{3,1,2,0:T(8,128)} fusion(f32[1,384,8,128]{3,1,2,0:T(8,128)} %get-tuple-element.220, f32[512,384,8]{1,0,2:T(8,128)S(1)} %get-tuple-element.204, f32[384,8]{0,1:T(8,128)S(1)} %bitcast.122, pred[384,512]{0,1:T(8,128)(4,1)S(1)} %compare_and_fusion.4, f32[384,8]{0,1:T(8,128)S(1)} %get-tuple-element.205, ...), kind=kOutput, calls=%fused_computation.7.clone.1 | convolution fusion | flops 411303936 | bytes 9789952 | tf_op jit(solution)/shard_map/while/body/eval_jaxpr/jtqk,kjd->jtqd/dot_general | solution.py:75
  293.9 4.4 %bitcast_add_fusion.6 = f32[1,384,8,128]{3,1,2,0:T(8,128)} fusion(f32[1,384,8,128]{3,1,2,0:T(8,128)} %get-tuple-element.220, f32[512,384,8]{1,0,2:T(8,128)S(1)} %get-tuple-element.204, f32[384,8]{0,1:T(8,128)S(1)} %bitcast.122, pred[384,512]{0,1:T(8,128)(4,1)S(1)} %compare_and_fusion.4, f32[384,8]{0,1:T(8,128)S(1)} %get-tuple-element.205, ...), kind=kOutput, calls=%fused_computation.7.clone.1 | convolution fusion | flops 411303936 | bytes 9789952 | tf_op jit(solution)/shard_map/while/body/eval_jaxpr/jtqk,kjd->jtqd/dot_general | solution.py:75
  308.4 4.4 %bitcast_add_fusion.6 = f32[1,384,8,128]{3,1,2,0:T(8,128)} fusion(f32[1,384,8,128]{3,1,2,0:T(8,128)} %get-tuple-element.220, f32[512,384,8]{1,0,2:T(8,128)S(1)} %get-tuple-element.204, f32[384,8]{0,1:T(8,128)S(1)} %bitcast.122, pred[384,512]{0,1:T(8,128)(4,1)S(1)} %compare_and_fusion.4, f32[384,8]{0,1:T(8,128)S(1)} %get-tuple-element.205, ...), kind=kOutput, calls=%fused_computation.7.clone.1 | convolution fusion | flops 411303936 | bytes 9789952 | tf_op jit(solution)/shard_map/while/body/eval_jaxpr/jtqk,kjd->jtqd/dot_general | solution.py:75
  323.0 4.4 %bitcast_add_fusion.6 = f32[1,384,8,128]{3,1,2,0:T(8,128)} fusion(f32[1,384,8,128]{3,1,2,0:T(8,128)} %get-tuple-element.220, f32[512,384,8]{1,0,2:T(8,128)S(1)} %get-tuple-element.204, f32[384,8]{0,1:T(8,128)S(1)} %bitcast.122, pred[384,512]{0,1:T(8,128)(4,1)S(1)} %compare_and_fusion.4, f32[384,8]{0,1:T(8,128)S(1)} %get-tuple-element.205, ...), kind=kOutput, calls=%fused_computation.7.clone.1 | convolution fusion | flops 411303936 | bytes 9789952 | tf_op jit(solution)/shard_map/while/body/eval_jaxpr/jtqk,kjd->jtqd/dot_general | solution.py:75
  330.3 4.4 %bitcast_add_fusion.6 = f32[1,384,8,128]{3,1,2,0:T(8,128)} fusion(f32[1,384,8,128]{3,1,2,0:T(8,128)} %get-tuple-element.220, f32[512,384,8]{1,0,2:T(8,128)S(1)} %get-tuple-element.204, f32[384,8]{0,1:T(8,128)S(1)} %bitcast.122, pred[384,512]{0,1:T(8,128)(4,1)S(1)} %compare_and_fusion.4, f32[384,8]{0,1:T(8,128)S(1)} %get-tuple-element.205, ...), kind=kOutput, calls=%fused_computation.7.clone.1 | convolution fusion | flops 411303936 | bytes 9789952 | tf_op jit(solution)/shard_map/while/body/eval_jaxpr/jtqk,kjd->jtqd/dot_general | solution.py:75
  (153 shorter events, 76.0 us)
Async XLA Ops:
  6.5 73.4 %all-gather.2.cloned.1.call-start = ((), (), s32[]{:S(2)}) async-start(), calls=%async_computation.1 | async-start | bytes 4325376 | tf_op jit(solution)/shard_map/all_gather | solution.py:104
  7.3 121.8 %collective-permute-start = (bf16[2,384,128]{2,1,0:T(8,128)(2,1)}, bf16[2,384,128]{2,1,0:T(8,128)(2,1)S(1)}, u32[]{:S(2)}, u32[]{:S(2)}) collective-permute-start(bf16[2,384,128]{2,1,0:T(8,128)(2,1)} %param.10), channel_id=1, source_target_pairs={{0,8},{8,16},{16,24},{24,32},{32,40},{40,48},{48,56},{56,64},{64,7... | collective-permute-start | bytes 589832 | tf_op jit(solution)/shard_map/ppermute | solution.py:20
  121.8 7.3 %copy-start.1 = (bf16[2,384,128]{2,1,0:T(8,128)(2,1)S(1)}, bf16[2,384,128]{2,1,0:T(8,128)(2,1)}, u32[]{:S(2)}) copy-start(bf16[2,384,128]{2,1,0:T(8,128)(2,1)} %param.10) | copy-start | bytes 589828
  121.8 7.3 %copy-start = (bf16[384,1024]{1,0:T(8,128)(2,1)S(1)}, bf16[384,1024]{1,0:T(8,128)(2,1)}, u32[]{:S(2)}) copy-start(bf16[384,1024]{1,0:T(8,128)(2,1)} %param.9) | copy-start | bytes 2359300
  121.8 55.0 %all-to-all-start = ((bf16[8,2,131072]{2,1,0:T(2,128)(2,1)}), bf16[8,2,131072]{2,1,0:T(2,128)(2,1)}, u32[]{:S(2)}, u32[]{:S(2)}) async-start(bf16[8,2,131072]{2,1,0:T(2,128)(2,1)} %reshape.344), calls=%async_computation | async-start | bytes 8388608 | tf_op jit(solution)/shard_map/all_to_all | solution.py:105
Sparse Core Ops, SparseCore 0:
  9.2 70.6 all-gather.1
where the time goes:
time: 348 us; the launch traced here: 347 us
  waiting for transfers between devices  105 us (30%)
  matrix products  93.4 us (27%)
  local copies, waits for them, and re-layouts  88.6 us (25%)
  other arithmetic  34.7 us (10%)
  between operations  13.6 us (4%)
  starting transfers between devices  10.8 us (3%)
    dot_general x17, matrix products, absorb(): jnp.einsum('jtqk,kjd->jtqd', weights.astype(jnp.bfloat16), value_rows, pr...  73.8 us
    all_gather x1, waiting for transfers between devices, per_device(): stored = lax.all_gather(prefix_kv, 'req', axis=1, tiled=True)  64.1 us
    all_to_all x1, waiting for transfers between devices, per_device(): lax.all_to_all(stored, 'tp', split_axis=3, concat_axis=2, tiled=True)  39.8 us
    unnamed x10, local copies, waits for them, and re-layouts  33.7 us
    reduce_sum x17, other arithmetic, absorb(): new_sum = running_sum * shrink + jnp.sum(weights, axis=-1)  26.4 us
    all_gather x1, local copies, waits for them, and re-layouts, per_device(): stored = lax.all_gather(prefix_kv, 'req', axis=1, tiled=True)  23.2 us
    slice x2, local copies, waits for them, and re-layouts, per_device(): value_rows = relaid[1].reshape(passes, stride * block_rows, kv_heads, HD)  21.9 us
    dot_general x17, matrix products, absorb(): jnp.einsum('tjqd,kjd->jtqk', query_heads, key_rows, preferred_element_typ...  19.6 us
  transfers between devices with their start and end apart: 3, of which 2 were waited for; matrix products, arithmetic and copies ran while one was open for 16% of the time, Pallas kernels for 0%

commit v1 on v0

v1 whole, which is shorter than its diff:
```python
import functools
import math

import jax
import jax.numpy as jnp
from jax import lax
from jax.experimental import pallas as pl
from jax.experimental.pallas import tpu as pltpu
from jax.sharding import PartitionSpec as P

QH = 64
KVH = 8
HD = 128
GROUPS = 4

masked_score = -1e30
TILE = 64
CHUNK = 512


def from_behind(block, axis, distance):
    devices = range(lax.axis_size(axis))
    route = [(i - distance, i) for i in devices if i - distance in devices]
    return lax.ppermute(block, axis, route)


def attend_kernel(
    scal_ref, q_ref, pk_ref, pv_ref, s0_ref, s1_ref, o_ref, *, per_kv, tiles_per_half, half
):
    h = pl.program_id(0)
    i = pl.program_id(1)
    base = scal_ref[0]
    start = jnp.where(h == 0, scal_ref[1], scal_ref[3])
    stop = jnp.where(h == 0, scal_ref[2], scal_ref[4])
    slot0 = base + h * half + i * TILE
    any_live = (start < slot0 + TILE) & (stop > slot0)
    rows = per_kv * TILE
    scale = 1.0 / math.sqrt(HD)

    @pl.when(jnp.logical_not(any_live))
    def _():
        o_ref[...] = jnp.zeros_like(o_ref)

    def body(s_ref, key_base, n_suffix):
        q = jnp.concatenate([q_ref[:, j * HD : (j + 1) * HD] for j in range(per_kv)], axis=0)
        row = lax.broadcasted_iota(jnp.int32, (rows, 1), 0)
        slot = slot0 + jnp.bitwise_and(row, TILE - 1)
        live = (slot >= start) & (slot < stop)
        key_slot = key_base + lax.broadcasted_iota(jnp.int32, (1, n_suffix), 1)
        suffix_ok = (key_slot >= start) & (key_slot <= slot) & live

        def scores(k):
            return (
                lax.dot_general(
                    q, k, (((1,), (1,)), ((), ())), preferred_element_type=jnp.float32
                )
                * scale
            )

        n_chunks = pk_ref.shape[0] // CHUNK

        def max_step(c, m):
            k = pk_ref[pl.ds(pl.multiple_of(c * CHUNK, CHUNK), CHUNK), :]
            s = jnp.where(live, scores(k), masked_score)
            return jnp.maximum(m, jnp.max(s, axis=1, keepdims=True))

        m = jnp.full((rows, 1), masked_score, jnp.float32)
        m = lax.fori_loop(0, n_chunks, max_step, m)
        s_suf = jnp.where(suffix_ok, scores(s_ref[0]), masked_score)
        m = jnp.maximum(m, jnp.max(s_suf, axis=1, keepdims=True))

        def sum_step(c, carry):
            l, acc = carry
            at = pl.ds(pl.multiple_of(c * CHUNK, CHUNK), CHUNK)
            s = scores(pk_ref[at, :])
            p = jnp.where(live, jnp.exp(s - m), 0.0)
            l = l + jnp.sum(p, axis=1, keepdims=True)
            acc = acc + jnp.dot(
                p.astype(jnp.bfloat16), pv_ref[at, :], preferred_element_type=jnp.float32
            )
            return (l, acc)

        l = jnp.zeros((rows, 1), jnp.float32)
        acc = jnp.zeros((rows, HD), jnp.float32)
        l, acc = lax.fori_loop(0, n_chunks, sum_step, (l, acc))
        p = jnp.where(suffix_ok, jnp.exp(s_suf - m), 0.0)
        l = l + jnp.sum(p, axis=1, keepdims=True)
        acc = acc + jnp.dot(p.astype(jnp.bfloat16), s_ref[1], preferred_element_type=jnp.float32)
        out = jnp.where(live, acc / jnp.where(live, l, 1.0), 0.0).astype(o_ref.dtype)
        for j in range(per_kv):
            o_ref[:, j * HD : (j + 1) * HD] = out[j * TILE : (j + 1) * TILE, :]

    @pl.when(any_live & (h == 0))
    def _():
        body(s0_ref, base - half, s0_ref.shape[1])

    @pl.when(any_live & (h == 1))
    def _():
        body(s1_ref, base + half, s1_ref.shape[1])


def per_device(
    queries, suffix_kv, prefix_kv, suffix_length, request_group, request_order, owner_map
):
    tok_rows = queries.shape[0]
    head_cols = suffix_kv.shape[2]
    kv_heads = head_cols // HD
    per_kv = queries.shape[1] // head_cols
    stored_count = owner_map.shape[0]
    per_group = stored_count // GROUPS
    requests = suffix_length.shape[0]
    half = tok_rows // 2
    packed_length = jnp.take(suffix_length, request_order)
    packed_group = jnp.take(request_group, request_order)
    starts = (jnp.arange(requests, dtype=jnp.int32) + 1) * tok_rows - packed_length // 2
    stops = starts + packed_length
    device = lax.axis_index("req")
    base = device * tok_rows
    first = jnp.clip(device - 1, 0, requests - 1)
    second = jnp.clip(device, 0, requests - 1)
    has_first = device >= 1
    has_second = device < requests
    start0 = jnp.where(has_first, starts[first], -1)
    stop0 = jnp.where(has_first, stops[first], -1)
    start1 = jnp.where(has_second, starts[second], -1)
    stop1 = jnp.where(has_second, stops[second], -1)
    scal = jnp.stack([base, start0, stop0, start1, stop1, base, base, base]).astype(jnp.int32)
    groups = jnp.stack([packed_group[first], packed_group[second]])
    rows_of = jnp.take(
        owner_map, groups[:, None] * per_group + jnp.arange(per_group, dtype=jnp.int32)[None, :]
    )

    local = lax.all_to_all(prefix_kv, "tp", split_axis=3, concat_axis=2, tiled=True)
    stored = lax.all_gather(local, "req", axis=1, tiled=True)
    block_rows = stored.shape[2]
    picked = jnp.take(stored, rows_of.reshape(-1), axis=1)
    picked = picked.reshape(2, 2, per_group * block_rows, HD)
    pk = picked[0]
    pv = picked[1]

    earlier = from_behind(suffix_kv[:, half:, :], "req", 1)
    s0 = jnp.concatenate([earlier, suffix_kv[:, :half, :]], axis=1)
    pad = (-half) % 128
    s1 = jnp.concatenate(
        [suffix_kv[:, half:, :], jnp.zeros((2, pad, head_cols), suffix_kv.dtype)], axis=1
    )

    tiles_per_half = half // TILE
    grid = (2, tiles_per_half)
    kernel = functools.partial(
        attend_kernel, per_kv=per_kv, tiles_per_half=tiles_per_half, half=half
    )
    prefix_rows = per_group * block_rows
    return pl.pallas_call(
        kernel,
        out_shape=jax.ShapeDtypeStruct((tok_rows, per_kv * HD), queries.dtype),
        grid_spec=pltpu.PrefetchScalarGridSpec(
            num_scalar_prefetch=1,
            grid=grid,
            in_specs=[
                pl.BlockSpec((TILE, per_kv * HD), lambda h, i, s: (h * tiles_per_half + i, 0)),
                pl.BlockSpec((None, prefix_rows, HD), lambda h, i, s: (h, 0, 0)),
                pl.BlockSpec((None, prefix_rows, HD), lambda h, i, s: (h, 0, 0)),
                pl.BlockSpec(s0.shape, lambda h, i, s: (0, 0, 0)),
                pl.BlockSpec(s1.shape, lambda h, i, s: (0, 0, 0)),
            ],
            out_specs=pl.BlockSpec((TILE, per_kv * HD), lambda h, i, s: (h * tiles_per_half + i, 0)),
        ),
        compiler_params=pltpu.CompilerParams(dimension_semantics=("arbitrary", "arbitrary")),
    )(scal, queries, pk, pv, s0, s1)


def solution(mesh):
    in_specs = (
        P("req", "tp"),
        P(None, "req", "tp"),
        P(None, "req", "tp", None),
        P(),
        P(),
        P(),
        P(),
    )
    out_specs = P("req", "tp")
    return jax.shard_map(
        per_device, mesh=mesh, in_specs=in_specs, out_specs=out_specs, check_vma=False
    )
```

time: 348 us -> 131 us (0.38)
  the two profiles are of different devices: /device:TPU:1 before, /device:TPU:97 now
where the time goes in v1:
time: 131 us
  waiting for transfers between devices  51.3 us (39%)
  Pallas kernels  30.9 us (24%)
  between operations  16.1 us (12%)
  blocking collectives  13.4 us (10%)
  local copies, waits for them, and re-layouts  12.8 us (10%)
  starting transfers between devices  4.24 us (3%)
  other arithmetic  2.29 us (2%)
    all_gather x1, waiting for transfers between devices, per_device(): stored = lax.all_gather(local, 'req', axis=1, tiled=True)  51.2 us
    pallas_call x1, Pallas kernels, per_device(): pl.pallas_call(kernel, out_shape=jax.ShapeDtypeStruct((tok_rows, per_kv *...  30.9 us
    all_to_all x1, blocking collectives, per_device(): lax.all_to_all(prefix_kv, 'tp', split_axis=3, concat_axis=2, tiled=True)  13.4 us
    ppermute x1, starting transfers between devices, from_behind(): return lax.ppermute(block, axis, route)  4.21 us
    gather x1, local copies, waits for them, and re-layouts, per_device(): picked = jnp.take(stored, rows_of.reshape(-1), axis=1)  3.14 us
  transfers between devices with their start and end apart: 2, of which 1 were waited for; matrix products, arithmetic and copies ran while one was open for 5% of the time, Pallas kernels for 0%

profile of v1, /device:TPU:97, one launch (start us, length us, event | category | flops | bytes accessed | tf_op | source)
XLA Modules:
  0.0 131.0 jit_solution(10457421526725924067)
XLA Ops:
  6.6 1.3 copy.15
  7.9 0.5 reshape.187
  8.4 13.4 %all_to_all.18 = bf16[8,2,4096]{2,1,0:T(2,128)(2,1)S(1)} all-to-all(bf16[8,2,4096]{2,1,0:T(2,128)(2,1)S(1)} %reshape.187), channel_id=1, replica_groups=mesh['req'=32,'tp'=8] {'tp'}, dimensions={0} | all-to-all | bytes 262144 | tf_op jit(solution)/shard_map/all_to_all | solution.py:133
  21.8 0.3 reshape.188
  22.0 1.0 copy.20
  23.1 4.2 %collective-permute-start = (bf16[2,192,128]{2,1,0:T(8,128)(2,1)S(1)}, bf16[2,192,128]{2,1,0:T(8,128)(2,1)S(1)}, u32[]{:S(2)}, u32[]{:S(2)}) collective-permute-start(bf16[2,192,128]{2,1,0:T(8,128)(2,1)S(1)} %get-tuple-element.12), channel_id=1, source_target_pairs={{0,8},{8,16},{16,24},{24,32},{32,40},{40,48},{48,56},{56,64},{64,7... | collective-permute-start | bytes 294920 | tf_op jit(solution)/shard_map/ppermute | solution.py:24
  27.3 0.7 gather_fusion.3
  28.1 0.6 fusion.6
  28.7 1.2 add_multiply_fusion
  29.9 0.1 add.124
  30.1 0.7 gather_fusion.2
  30.8 0.7 fusion.7
  34.1 0.1 reshape.164
  34.2 0.1 add.126
  34.3 0.1 add.116
  34.4 0.7 concatenate.11.s1_ref
  35.1 0.7 gather_fusion
  35.7 0.6 stack.29.scal_ref
  36.4 0.7 pad_maximum_fusion.s0_ref
  37.1 51.2 %all-gather.2.cloned.1.call-done = bf16[2,32,256,128]{3,2,1,0:T(8,128)(2,1)} async-done(((bf16[2,1,256,128]{3,2,1,0:T(8,128)(2,1)}), bf16[2,32,256,128]{3,2,1,0:T(8,128)(2,1)}) %all-gather.2.cloned.1.call-update) | async-done | bytes 4194320 | tf_op jit(solution)/shard_map/all_gather | solution.py:134
  88.3 3.1 %gather_fusion.1 = bf16[16,2,256,128]{3,2,1,0:T(8,128)(2,1)S(1)} fusion(bf16[2,32,256,128]{3,2,1,0:T(8,128)(2,1)} %all-gather.2.cloned.1.call-done, s32[1024]{0:T(1024)S(1)} %pad_clamp_fusion), kind=kCustom, calls=%fused_computation.3 | custom fusion | bytes 4194368 | tf_op jit(solution)/shard_map/jit(_take)/gather | solution.py:136
  91.5 0.3 select_bitcast_fusion
  91.7 1.5 %fusion.4 = (bf16[1,16,256,128]{3,2,0,1:T(8,128)(2,1)}, bf16[1,16,256,128]{3,2,0,1:T(8,128)(2,1)}) fusion(bf16[2,16,256,128]{3,2,0,1:T(8,128)(2,1)S(1)} %select_bitcast_fusion), kind=kLoop, calls=%fused_computation.29 | loop fusion | bytes 4194304 | tf_op jit(solution)/shard_map/slice | solution.py:139
  93.2 30.9 %shard_map.73 = bf16[384,1024]{1,0:T(8,128)(2,1)} custom-call(s32[8]{0:T(128)} %stack.29.scal_ref, bf16[384,1024]{1,0:T(8,128)(2,1)} %q_ref.1, bf16[2,2048,128]{2,1,0:T(8,128)(2,1)} %bitcast.35, bf16[2,2048,128]{2,1,0:T(8,128)(2,1)} %bitcast.34, bf16[2,384,128]{2,1,0:T(8,128)(2,1)} %pad_maximum_fusion.s0_ref, bf16[2,256,128]{2,1,0:T(8,128)(2,1)} %concatenate.11.s1_ref), custom_call_target="tpu_custom_call" | custom-call | tf_op jit(solution)/shard_map/pallas_call | solution.py:154
  (27 shorter events, 0.4 us)
Async XLA Ops:
  6.5 20.8 %copy-start = (s32[31]{0:T(128)S(1)}, s32[31]{0:T(128)}, u32[]{:S(2)}) copy-start(s32[31]{0:T(128)} %param.13) | copy-start | bytes 376
  6.5 16.5 %copy-start.3 = (bf16[2,384,128]{2,1,0:T(8,128)(2,1)S(1)}, bf16[2,384,128]{2,1,0:T(8,128)(2,1)}, u32[]{:S(2)}) copy-start(bf16[2,384,128]{2,1,0:T(8,128)(2,1)} %param.10) | copy-start | bytes 589828
  6.5 20.8 %copy-start.4 = (s32[31]{0:T(128)S(1)}, s32[31]{0:T(128)}, u32[]{:S(2)}) copy-start(s32[31]{0:T(128)} %param.14) | copy-start | bytes 376
  6.5 23.5 %copy-start.2 = (s32[31]{0:T(128)S(1)}, s32[31]{0:T(128)}, u32[]{:S(2)}) copy-start(s32[31]{0:T(128)} %param.12) | copy-start | bytes 376
  6.5 81.8 %all-gather.2.cloned.1.call-start = ((), (), s32[]{:S(2)}) async-start(), calls=%async_computation.1 | async-start | bytes 4325376 | tf_op jit(solution)/shard_map/all_gather | solution.py:134
  7.9 27.2 %copy-start.1 = (s32[32]{0:T(128)S(1)}, s32[32]{0:T(128)}, u32[]{:S(2)}) copy-start(s32[32]{0:T(128)} %param.15) | copy-start | bytes 388
  23.1 13.3 %collective-permute-start = (bf16[2,192,128]{2,1,0:T(8,128)(2,1)S(1)}, bf16[2,192,128]{2,1,0:T(8,128)(2,1)S(1)}, u32[]{:S(2)}, u32[]{:S(2)}) collective-permute-start(bf16[2,192,128]{2,1,0:T(8,128)(2,1)S(1)} %get-tuple-element.12), channel_id=1, source_target_pairs={{0,8},{8,16},{16,24},{24,32},{32,40},{40,48},{48,56},{56,64},{64,7... | collective-permute-start | bytes 294920 | tf_op jit(solution)/shard_map/ppermute | solution.py:24
Sparse Core Ops, SparseCore 0:
  23.2 65.1 all-gather.1

commit v2 on v1

--- a/solution.py
+++ b/solution.py
@@ -114,7 +114,7 @@
     packed_group = jnp.take(request_group, request_order)
     starts = (jnp.arange(requests, dtype=jnp.int32) + 1) * tok_rows - packed_length // 2
     stops = starts + packed_length
-    device = lax.axis_index("req")
+    device = lax.axis_index(("chip", "core"))
     base = device * tok_rows
     first = jnp.clip(device - 1, 0, requests - 1)
     second = jnp.clip(device, 0, requests - 1)
@@ -130,15 +130,30 @@
         owner_map, groups[:, None] * per_group + jnp.arange(per_group, dtype=jnp.int32)[None, :]
     )
 
-    local = lax.all_to_all(prefix_kv, "tp", split_axis=3, concat_axis=2, tiled=True)
-    stored = lax.all_gather(local, "req", axis=1, tiled=True)
+    tp = lax.axis_index("tp")
+    n_tp = lax.axis_size("tp")
+    pieces = []
+    for k in range(n_tp):
+        col = ((tp + k) % n_tp) * HD
+        piece = lax.dynamic_slice_in_dim(prefix_kv, col, HD, axis=3)
+        if k:
+            piece = lax.ppermute(piece, "tp", [(j, (j + k) % n_tp) for j in range(n_tp)])
+        pieces.append(piece)
+    local = jnp.concatenate(pieces, axis=2)
+    own = lax.all_gather(local, "chip", axis=1, tiled=True)
+    other = lax.ppermute(own, "core", [(0, 1), (1, 0)])
+    stored = jnp.concatenate([own, other], axis=1)
+    per_chip = own.shape[1]
     block_rows = stored.shape[2]
-    picked = jnp.take(stored, rows_of.reshape(-1), axis=1)
+    core = lax.axis_index("core")
+    flat = rows_of.reshape(-1)
+    where_stored = jnp.where(flat % 2 == core, 0, per_chip) + flat // 2
+    picked = jnp.take(stored, where_stored, axis=1)
     picked = picked.reshape(2, 2, per_group * block_rows, HD)
     pk = picked[0]
     pv = picked[1]
 
-    earlier = from_behind(suffix_kv[:, half:, :], "req", 1)
+    earlier = from_behind(suffix_kv[:, half:, :], ("chip", "core"), 1)
     s0 = jnp.concatenate([earlier, suffix_kv[:, :half, :]], axis=1)
     pad = (-half) % 128
     s1 = jnp.concatenate(
@@ -171,16 +186,20 @@
 
 
 def solution(mesh):
+    devices = mesh.devices
+    n_req, n_tp = devices.shape
+    split = jax.sharding.Mesh(devices.reshape(n_req // 2, 2, n_tp), ("chip", "core", "tp"))
+    req = ("chip", "core")
     in_specs = (
-        P("req", "tp"),
-        P(None, "req", "tp"),
-        P(None, "req", "tp", None),
-        P(),
-        P(),
-        P(),
-        P(),
-    )
-    out_specs = P("req", "tp")
+        P(req, "tp"),
+        P(None, req, "tp"),
+        P(None, req, "tp", None),
+        P(),
+        P(),
+        P(),
+        P(),
+    )
+    out_specs = P(req, "tp")
     return jax.shard_map(
-        per_device, mesh=mesh, in_specs=in_specs, out_specs=out_specs, check_vma=False
-    )
+        per_device, mesh=split, in_specs=in_specs, out_specs=out_specs, check_vma=False
+    )

time: 131 us -> 162 us (1.24)
  the two profiles are of different devices: /device:TPU:97 before, /device:TPU:109 now
where the time goes in v2:
time: 162 us; the launch traced here: 160 us
  waiting for transfers between devices  70.1 us (43%)
  Pallas kernels  27.3 us (17%)
  starting transfers between devices  25.9 us (16%)
  between operations  16.2 us (10%)
  local copies, waits for them, and re-layouts  12.3 us (8%)
  other arithmetic  7.66 us (5%)
    all_gather x1, waiting for transfers between devices, per_device(): own = lax.all_gather(local, 'chip', axis=1, tiled=True)  69 us
    pallas_call x1, Pallas kernels, per_device(): pl.pallas_call(kernel, out_shape=jax.ShapeDtypeStruct((tok_rows, per_kv *...  27.3 us
    ppermute x7, starting transfers between devices, per_device(): lax.ppermute(piece, 'tp', [(j, (j + k) % n_tp) for j in range(n_tp)])  11.5 us
    ppermute x1, starting transfers between devices, per_device(): other = lax.ppermute(own, 'core', [(0, 1), (1, 0)])  9.67 us
    ppermute x1, starting transfers between devices, from_behind(): return lax.ppermute(block, axis, route)  4.75 us
    concatenate x1, other arithmetic, per_device(): stored = jnp.concatenate([own, other], axis=1)  3.89 us
  transfers between devices with their start and end apart: 10, of which 3 were waited for; matrix products, arithmetic and copies ran while one was open for 6% of the time, Pallas kernels for 0%

profile of v2, /device:TPU:109, one launch (start us, length us, event | category | flops | bytes accessed | tf_op | source)
XLA Modules:
  0.0 159.5 jit_solution(8585171192012989109)
XLA Ops:
  6.7 0.9 constant_dynamic-slice_fusion
  7.5 1.4 collective-permute-start
  8.9 0.8 collective-permute-start.1
  9.7 1.9 %collective-permute-start.2 = (bf16[2,1,32,128]{3,2,1,0:T(8,128)(2,1)S(1)}, bf16[2,1,32,128]{3,2,1,0:T(8,128)(2,1)S(1)}, u32[]{:S(2)}, u32[]{:S(2)}) collective-permute-start(bf16[2,1,32,128]{3,2,1,0:T(8,128)(2,1)S(1)} %get-tuple-element.17), channel_id=1, source_target_pairs={{0,3},{1,4},{2,5},{3,6},{4,7},{5,0},{6,1},{7,2},{8,11},{9,12},{10,... | collective-permute-start | bytes 49160 | tf_op jit(solution)/shard_map/ppermute | solution.py:140
  11.6 2.7 %collective-permute-start.3 = (bf16[2,1,32,128]{3,2,1,0:T(8,128)(2,1)S(1)}, bf16[2,1,32,128]{3,2,1,0:T(8,128)(2,1)S(1)}, u32[]{:S(2)}, u32[]{:S(2)}) collective-permute-start(bf16[2,1,32,128]{3,2,1,0:T(8,128)(2,1)S(1)} %get-tuple-element.16), channel_id=1, source_target_pairs={{0,4},{1,5},{2,6},{3,7},{4,0},{5,1},{6,2},{7,3},{8,12},{9,13},{10,... | collective-permute-start | bytes 49160 | tf_op jit(solution)/shard_map/ppermute | solution.py:140
  14.4 1.7 %collective-permute-start.4 = (bf16[2,1,32,128]{3,2,1,0:T(8,128)(2,1)S(1)}, bf16[2,1,32,128]{3,2,1,0:T(8,128)(2,1)S(1)}, u32[]{:S(2)}, u32[]{:S(2)}) collective-permute-start(bf16[2,1,32,128]{3,2,1,0:T(8,128)(2,1)S(1)} %get-tuple-element.15), channel_id=1, source_target_pairs={{0,5},{1,6},{2,7},{3,0},{4,1},{5,2},{6,3},{7,4},{8,13},{9,14},{10,... | collective-permute-start | bytes 49160 | tf_op jit(solution)/shard_map/ppermute | solution.py:140
  16.1 1.1 collective-permute-start.5
  17.2 1.9 %collective-permute-start.6 = (bf16[2,1,32,128]{3,2,1,0:T(8,128)(2,1)S(1)}, bf16[2,1,32,128]{3,2,1,0:T(8,128)(2,1)S(1)}, u32[]{:S(2)}, u32[]{:S(2)}) collective-permute-start(bf16[2,1,32,128]{3,2,1,0:T(8,128)(2,1)S(1)} %get-tuple-element.14), channel_id=1, source_target_pairs={{0,7},{1,0},{2,1},{3,2},{4,3},{5,4},{6,5},{7,6},{8,15},{9,8},{10,9... | collective-permute-start | bytes 49160 | tf_op jit(solution)/shard_map/ppermute | solution.py:140
  19.4 0.8 collective-permute-done.5
  20.9 69.0 %all-gather.2.cloned.1.call-done = bf16[2,16,256,128]{3,2,1,0:T(8,128)(2,1)} async-done(((bf16[2,1,256,128]{3,2,1,0:T(8,128)(2,1)}), bf16[2,16,256,128]{3,2,1,0:T(8,128)(2,1)}) %all-gather.2.cloned.1.call-update) | async-done | bytes 2097168 | tf_op jit(solution)/shard_map/all_gather | solution.py:143
  89.9 9.7 %collective-permute-start.7 = (bf16[2,16,256,128]{3,2,1,0:T(8,128)(2,1)}, bf16[2,16,256,128]{3,2,1,0:T(8,128)(2,1)}, u32[]{:S(2)}, u32[]{:S(2)}) collective-permute-start(bf16[2,16,256,128]{3,2,1,0:T(8,128)(2,1)} %all-gather.2.cloned.1.call-done), channel_id=1, source_target_pairs={{0,8},{8,0},{1,9},{9,1},{2,10},{10,2},{3,11},{11,3},{4,12},{12,4},... | collective-permute-start | bytes 6291464 | tf_op jit(solution)/shard_map/ppermute | solution.py:144
  99.6 1.0 fusion.7
  100.5 4.8 %collective-permute-start.8 = (bf16[2,192,128]{2,1,0:T(8,128)(2,1)S(1)}, bf16[2,192,128]{2,1,0:T(8,128)(2,1)S(1)}, u32[]{:S(2)}, u32[]{:S(2)}) collective-permute-start(bf16[2,192,128]{2,1,0:T(8,128)(2,1)S(1)} %get-tuple-element.12), channel_id=1, source_target_pairs={{0,8},{8,16},{16,24},{24,32},{32,40},{40,48},{48,56},{56,64},{64,7... | collective-permute-start | bytes 294920 | tf_op jit(solution)/shard_map/ppermute | solution.py:24
  106.0 0.7 gather_fusion.3
  106.7 0.7 broadcast_select_fusion
  108.0 1.3 add_multiply_fusion
  109.9 0.7 gather_fusion.2
  110.6 0.7 fusion.9
  113.9 0.7 concatenate.19.s1_ref
  115.9 0.7 pad_maximum_fusion.1.s0_ref
  116.6 3.9 %pad_maximum_fusion = bf16[2,32,256,128]{3,2,1,0:T(8,128)(2,1)} fusion(bf16[2,16,256,128]{3,2,1,0:T(8,128)(2,1)} %collective-permute-done.7, bf16[2,16,256,128]{3,2,1,0:T(8,128)(2,1)S(1)} %copy-done.3), kind=kLoop, calls=%fused_computation.4 | loop fusion | flops 2097152 | bytes 8388608 | tf_op jit(solution)/shard_map/concatenate | solution.py:145
  120.5 3.1 %gather_fusion.1 = bf16[16,2,256,128]{3,2,1,0:T(8,128)(2,1)S(1)} fusion(bf16[2,32,256,128]{3,2,1,0:T(8,128)(2,1)} %pad_maximum_fusion, s32[1024]{0:T(1024)S(1)} %pad_clamp_fusion), kind=kCustom, calls=%fused_computation.3 | custom fusion | bytes 4194368 | tf_op jit(solution)/shard_map/jit(_take)/gather | solution.py:151
  123.9 1.5 fusion.6
  125.4 27.3 %shard_map.73 = bf16[384,1024]{1,0:T(8,128)(2,1)} custom-call(s32[8]{0:T(128)} %stack.29.scal_ref, bf16[384,1024]{1,0:T(8,128)(2,1)} %q_ref.1, bf16[2,2048,128]{2,1,0:T(8,128)(2,1)} %bitcast.26, bf16[2,2048,128]{2,1,0:T(8,128)(2,1)} %bitcast.25, bf16[2,384,128]{2,1,0:T(8,128)(2,1)} %pad_maximum_fusion.1.s0_ref, bf16[2,256,128]{2,1,0:T(8,128)(2,1)} %concatenate.19.s1_ref), custom_call_target="tpu_custom_call" | custom-call | tf_op jit(solution)/shard_map/pallas_call | solution.py:169
  (47 shorter events, 4.5 us)
Async XLA Ops:
  6.5 99.5 %copy-start = (s32[31]{0:T(128)S(1)}, s32[31]{0:T(128)}, u32[]{:S(2)}) copy-start(s32[31]{0:T(128)} %param.13) | copy-start | bytes 376
  6.5 103.4 %copy-start.2 = (s32[31]{0:T(128)S(1)}, s32[31]{0:T(128)}, u32[]{:S(2)}) copy-start(s32[31]{0:T(128)} %param.12) | copy-start | bytes 376
  6.5 108.1 %copy-start.1 = (s32[32]{0:T(128)S(1)}, s32[32]{0:T(128)}, u32[]{:S(2)}) copy-start(s32[32]{0:T(128)} %param.15) | copy-start | bytes 388
  6.5 83.4 %all-gather.2.cloned.1.call-start = ((), (), s32[]{:S(2)}) async-start(), calls=%async_computation | async-start | bytes 2228224 | tf_op jit(solution)/shard_map/all_gather | solution.py:143
  7.5 8.6 %collective-permute-start = (bf16[2,1,32,128]{3,2,1,0:T(8,128)(2,1)S(1)}, bf16[2,1,32,128]{3,2,1,0:T(8,128)(2,1)S(1)}, u32[]{:S(2)}, u32[]{:S(2)}) collective-permute-start(bf16[2,1,32,128]{3,2,1,0:T(8,128)(2,1)S(1)} %get-tuple-element.19), channel_id=1, source_target_pairs={{0,1},{1,2},{2,3},{3,4},{4,5},{5,6},{6,7},{7,0},{8,9},{9,10},{10,1... | collective-permute-start | bytes 49160 | tf_op jit(solution)/shard_map/ppermute | solution.py:140
  8.9 8.3 %collective-permute-start.1 = (bf16[2,1,32,128]{3,2,1,0:T(8,128)(2,1)S(1)}, bf16[2,1,32,128]{3,2,1,0:T(8,128)(2,1)S(1)}, u32[]{:S(2)}, u32[]{:S(2)}) collective-permute-start(bf16[2,1,32,128]{3,2,1,0:T(8,128)(2,1)S(1)} %get-tuple-element.18), channel_id=1, source_target_pairs={{0,2},{1,3},{2,4},{3,5},{4,6},{5,7},{6,0},{7,1},{8,10},{9,11},{10,... | collective-permute-start | bytes 49160 | tf_op jit(solution)/shard_map/ppermute | solution.py:140
  9.7 9.4 %collective-permute-start.2 = (bf16[2,1,32,128]{3,2,1,0:T(8,128)(2,1)S(1)}, bf16[2,1,32,128]{3,2,1,0:T(8,128)(2,1)S(1)}, u32[]{:S(2)}, u32[]{:S(2)}) collective-permute-start(bf16[2,1,32,128]{3,2,1,0:T(8,128)(2,1)S(1)} %get-tuple-element.17), channel_id=1, source_target_pairs={{0,3},{1,4},{2,5},{3,6},{4,7},{5,0},{6,1},{7,2},{8,11},{9,12},{10,... | collective-permute-start | bytes 49160 | tf_op jit(solution)/shard_map/ppermute | solution.py:140
  11.6 7.4 %collective-permute-start.3 = (bf16[2,1,32,128]{3,2,1,0:T(8,128)(2,1)S(1)}, bf16[2,1,32,128]{3,2,1,0:T(8,128)(2,1)S(1)}, u32[]{:S(2)}, u32[]{:S(2)}) collective-permute-start(bf16[2,1,32,128]{3,2,1,0:T(8,128)(2,1)S(1)} %get-tuple-element.16), channel_id=1, source_target_pairs={{0,4},{1,5},{2,6},{3,7},{4,0},{5,1},{6,2},{7,3},{8,12},{9,13},{10,... | collective-permute-start | bytes 49160 | tf_op jit(solution)/shard_map/ppermute | solution.py:140
  14.4 5.0 %collective-permute-start.4 = (bf16[2,1,32,128]{3,2,1,0:T(8,128)(2,1)S(1)}, bf16[2,1,32,128]{3,2,1,0:T(8,128)(2,1)S(1)}, u32[]{:S(2)}, u32[]{:S(2)}) collective-permute-start(bf16[2,1,32,128]{3,2,1,0:T(8,128)(2,1)S(1)} %get-tuple-element.15), channel_id=1, source_target_pairs={{0,5},{1,6},{2,7},{3,0},{4,1},{5,2},{6,3},{7,4},{8,13},{9,14},{10,... | collective-permute-start | bytes 49160 | tf_op jit(solution)/shard_map/ppermute | solution.py:140
  16.1 4.1 %collective-permute-start.5 = (bf16[2,1,32,128]{3,2,1,0:T(8,128)(2,1)S(1)}, bf16[2,1,32,128]{3,2,1,0:T(8,128)(2,1)S(1)}, u32[]{:S(2)}, u32[]{:S(2)}) collective-permute-start(bf16[2,1,32,128]{3,2,1,0:T(8,128)(2,1)S(1)} %get-tuple-element.21), channel_id=1, source_target_pairs={{0,6},{1,7},{2,0},{3,1},{4,2},{5,3},{6,4},{7,5},{8,14},{9,15},{10,... | collective-permute-start | bytes 49160 | tf_op jit(solution)/shard_map/ppermute | solution.py:140
  17.2 3.0 %collective-permute-start.6 = (bf16[2,1,32,128]{3,2,1,0:T(8,128)(2,1)S(1)}, bf16[2,1,32,128]{3,2,1,0:T(8,128)(2,1)S(1)}, u32[]{:S(2)}, u32[]{:S(2)}) collective-permute-start(bf16[2,1,32,128]{3,2,1,0:T(8,128)(2,1)S(1)} %get-tuple-element.14), channel_id=1, source_target_pairs={{0,7},{1,0},{2,1},{3,2},{4,3},{5,4},{6,5},{7,6},{8,15},{9,8},{10,9... | collective-permute-start | bytes 49160 | tf_op jit(solution)/shard_map/ppermute | solution.py:140
  20.2 0.7 copy-start.4
  89.9 26.7 %copy-start.3 = (bf16[2,16,256,128]{3,2,1,0:T(8,128)(2,1)S(1)}, bf16[2,16,256,128]{3,2,1,0:T(8,128)(2,1)}, u32[]{:S(2)}) copy-start(bf16[2,16,256,128]{3,2,1,0:T(8,128)(2,1)} %all-gather.2.cloned.1.call-done) | copy-start | bytes 6291460
  89.9 26.7 %collective-permute-start.7 = (bf16[2,16,256,128]{3,2,1,0:T(8,128)(2,1)}, bf16[2,16,256,128]{3,2,1,0:T(8,128)(2,1)}, u32[]{:S(2)}, u32[]{:S(2)}) collective-permute-start(bf16[2,16,256,128]{3,2,1,0:T(8,128)(2,1)} %all-gather.2.cloned.1.call-done), channel_id=1, source_target_pairs={{0,8},{8,0},{1,9},{9,1},{2,10},{10,2},{3,11},{11,3},{4,12},{12,4},... | collective-permute-start | bytes 6291464 | tf_op jit(solution)/shard_map/ppermute | solution.py:144
  100.5 15.3 %collective-permute-start.8 = (bf16[2,192,128]{2,1,0:T(8,128)(2,1)S(1)}, bf16[2,192,128]{2,1,0:T(8,128)(2,1)S(1)}, u32[]{:S(2)}, u32[]{:S(2)}) collective-permute-start(bf16[2,192,128]{2,1,0:T(8,128)(2,1)S(1)} %get-tuple-element.12), channel_id=1, source_target_pairs={{0,8},{8,16},{16,24},{24,32},{32,40},{40,48},{48,56},{56,64},{64,7... | collective-permute-start | bytes 294920 | tf_op jit(solution)/shard_map/ppermute | solution.py:24
Sparse Core Ops, SparseCore 0:
  21.0 68.8 all-gather.1
